TPU v7x, 256 devices: a whole 4x4x8 slice. The times are simulated.
256 devices in a mesh: dp: 32 (over x, y, core), mp: 8 (over z).
Axes of the slice: x: 4, y: 4, z: 8, core: 2. Of those that a mesh axis runs over, the one named last changes fastest.
Arguments:
- hidden: bfloat16 [512, 1024], P('dp'), may hold values from -6 to 6
- attn_gain: float32 [1024], replicated, may hold values from 0.25 to 1.75
- w_qkv: bfloat16 [1024, 3, 1024], P(None, None, 'mp'), may hold values from -2 to 2
- w_out: bfloat16 [1024, 1024], P('mp'), may hold values from -0.1875 to 0.1875
- mlp_gain: float32 [1024], replicated, may hold values from 0.25 to 1.75
- w_gate_up: bfloat16 [1024, 2, 4096], P(None, None, 'mp'), may hold values from -0.1875 to 0.1875
- w_down: bfloat16 [4096, 1024], P('mp'), may hold values from -0.09375 to 0.09375
- kv_cache: bfloat16 [2, 4096, 128, 1024], P(None, 'dp', None, 'mp'), may hold values from -9 to 9
- lengths: int32 [512], replicated, may hold values from 1 to 16384, as said below
- page_request: int32 [4096], P('dp'), may hold values from -1 to 511, as said below
- page_index: int32 [4096], P('dp'), may hold values from 0 to 127, as said below
Outputs:
- appended: bfloat16 [2, 512, 1024], P(None, 'dp', 'mp')
- hidden_out: bfloat16 [512, 1024], P('dp')
Inputs may be any that keep to these rules, and one draw needn't show every extreme that they name: `lengths`: 4 requests hold exactly 16384 tokens, the others fewer than 512. `page_request`: each request owns exactly ceil(lengths / 128) pool pages, which may lie on any data devices; -1 marks an empty page. `page_index`: the pages of a request carry the places 0 to ceil(lengths / 128) - 1, each once; empty pages carry 0.
All inputs are finite; a program needn't handle non-finite values.
Results may differ from a plain program's by a relative error of at most 0.0085.
Values may be sent and summed in bfloat16 or wider, within the bound.
No kernel may reach another device: no remote copies, remote signals or barrier semaphores. Data moves between devices by JAX's collectives and lax.ppermute only.
A program may use at most 128 MiB of HBM per device.

v0:
```python
import jax
import jax.numpy as jnp
from jax import lax
from jax.sharding import PartitionSpec as P

HEAD_DIM = 64
PAGE_BLOCK = 8
EPSILON = 1e-05
NEGATIVE = -1e30


def merged_2(value, axis, join):
    pieces = jax.tree.map(lambda part: lax.all_gather(part, axis), value)
    head = jax.tree.map(lambda part: part[0], pieces)
    tail = jax.tree.map(lambda part: part[1:], pieces)
    running, _ = lax.scan(lambda running, piece: (join(running, piece), None), head, tail)
    return running


def rms_norm(values, gain):
    widened = values.astype(jnp.float32)
    mean_square = jnp.mean(widened * widened, axis=-1, keepdims=True)
    return (widened * lax.rsqrt(mean_square + EPSILON) * gain).astype(jnp.bfloat16)


def combine(first, second):
    largest = jnp.maximum(first[0], second[0])
    shrink_first = jnp.exp(first[0] - largest)
    shrink_second = jnp.exp(second[0] - largest)
    totals = first[1] * shrink_first + second[1] * shrink_second
    weighted = first[2] * shrink_first[:, :, None] + second[2] * shrink_second[:, :, None]
    return (largest, totals, weighted)


def body(
    hidden,
    attn_gain,
    w_qkv,
    w_out,
    mlp_gain,
    w_gate_up,
    w_down,
    kv_cache,
    lengths,
    page_request,
    page_index,
):
    local_rows = hidden.shape[0]
    head_cols = w_qkv.shape[2]
    local_heads = head_cols // HEAD_DIM
    pool_pages = kv_cache.shape[1]
    page_len = kv_cache.shape[2]
    data_devices = lax.axis_size("dp")
    requests = local_rows * data_devices
    score_scale = HEAD_DIM ** (-0.5)
    normed = rms_norm(hidden, attn_gain)
    projected = jnp.dot(
        normed, w_qkv.reshape(w_qkv.shape[0], 3 * head_cols), preferred_element_type=jnp.float32
    )
    projected = lax.optimization_barrier(projected.astype(jnp.bfloat16)).reshape(
        local_rows, 3, head_cols
    )
    appended = jnp.stack([projected[:, 1], projected[:, 2]])
    every_query = lax.all_gather(projected[:, 0], "dp", axis=0, tiled=True)
    own_queries = projected[:, 0].reshape(local_rows, local_heads, HEAD_DIM).astype(jnp.float32)
    own_keys = projected[:, 1].reshape(local_rows, local_heads, HEAD_DIM).astype(jnp.float32)
    own_values = projected[:, 2].reshape(local_rows, local_heads, HEAD_DIM).astype(jnp.float32)
    self_scores = jnp.sum(own_queries * own_keys, axis=-1) * score_scale
    home_row = lax.axis_index("dp") * local_rows
    start_max = lax.dynamic_update_slice(
        jnp.full((requests, local_heads), NEGATIVE, jnp.float32), self_scores, (home_row, 0)
    )
    start_totals = lax.dynamic_update_slice(
        jnp.zeros((requests, local_heads), jnp.float32),
        jnp.ones((local_rows, local_heads), jnp.float32),
        (home_row, 0),
    )
    start_weighted = lax.dynamic_update_slice(
        jnp.zeros((requests, local_heads, HEAD_DIM), jnp.float32), own_values, (home_row, 0, 0)
    )
    visit_order = jnp.arange(pool_pages, dtype=jnp.int32)
    trip_count = pool_pages // PAGE_BLOCK
    request_ids = jnp.arange(requests, dtype=jnp.int32)
    offsets = jnp.arange(page_len, dtype=jnp.int32)

    def visit(step_index, carry):
        running_max, totals, weighted = carry
        picked = lax.dynamic_slice_in_dim(visit_order, step_index * PAGE_BLOCK, PAGE_BLOCK, 0)
        fetched = jnp.take(kv_cache, picked, axis=1)
        owners = page_request[picked]
        page_pos = page_index[picked]
        clamped = jnp.maximum(owners, 0)
        chosen_queries = every_query[clamped].reshape(PAGE_BLOCK, local_heads, HEAD_DIM)
        key_rows = fetched[0].reshape(PAGE_BLOCK, page_len, local_heads, HEAD_DIM)
        value_rows = fetched[1].reshape(PAGE_BLOCK, page_len, local_heads, HEAD_DIM)
        scores = (
            jnp.einsum(
                "phd,pthd->pht", chosen_queries, key_rows, preferred_element_type=jnp.float32
            )
            * score_scale
        )
        position = page_pos[:, None] * page_len + offsets[None, :]
        usable = (owners[:, None] >= 0) & (position < lengths[clamped][:, None])
        page_max = jnp.max(jnp.where(usable[:, None, :], scores, NEGATIVE), axis=2)
        raw = jnp.where(usable[:, None, :], jnp.exp(scores - page_max[:, :, None]), 0.0)
        page_total = jnp.sum(raw, axis=2)
        page_sum = jnp.einsum(
            "pht,pthd->phd",
            raw.astype(jnp.bfloat16),
            value_rows,
            preferred_element_type=jnp.float32,
        )
        member = owners[:, None] == request_ids[None, :]
        candidate = jnp.max(jnp.where(member[:, :, None], page_max[:, None, :], NEGATIVE), axis=0)
        new_max = jnp.maximum(running_max, candidate)
        factors = jnp.where(owners[:, None] >= 0, jnp.exp(page_max - new_max[clamped]), 0.0)
        rescale = jnp.exp(running_max - new_max)
        onehot = member.astype(jnp.float32)
        totals = totals * rescale + jnp.einsum(
            "pr,ph->rh", onehot, page_total * factors, precision=lax.Precision.HIGHEST
        )
        weighted = weighted * rescale[:, :, None] + jnp.einsum(
            "pr,phd->rhd", onehot, page_sum * factors[:, :, None], precision=lax.Precision.HIGHEST
        )
        return (new_max, totals, weighted)

    running_max, totals, weighted = lax.fori_loop(
        0, trip_count, visit, (start_max, start_totals, start_weighted)
    )
    merged = merged_2((running_max, totals, weighted), "dp", combine)
    own_totals = lax.dynamic_slice_in_dim(merged[1], home_row, local_rows, 0)
    own_weighted = lax.dynamic_slice_in_dim(merged[2], home_row, local_rows, 0)
    context = (
        (own_weighted / own_totals[:, :, None]).reshape(local_rows, head_cols).astype(jnp.bfloat16)
    )
    attended = lax.psum(jnp.dot(context, w_out, preferred_element_type=jnp.float32), "mp")
    residual = lax.optimization_barrier(
        (hidden.astype(jnp.float32) + attended).astype(jnp.bfloat16)
    )
    normed_mlp = rms_norm(residual, mlp_gain)
    hidden_cols = w_gate_up.shape[2]
    gate_up = jnp.dot(
        normed_mlp,
        w_gate_up.reshape(w_gate_up.shape[0], 2 * hidden_cols),
        preferred_element_type=jnp.float32,
    ).reshape(local_rows, 2, hidden_cols)
    activated = (jax.nn.silu(gate_up[:, 0]) * gate_up[:, 1]).astype(jnp.bfloat16)
    lowered = lax.psum(jnp.dot(activated, w_down, preferred_element_type=jnp.float32), "mp")
    hidden_out = (residual.astype(jnp.float32) + lowered).astype(jnp.bfloat16)
    return (appended, hidden_out)


def solution(mesh):
    return jax.shard_map(
        body,
        mesh=mesh,
        in_specs=(
            P("dp", None),
            P(),
            P(None, None, "mp"),
            P("mp", None),
            P(),
            P(None, None, "mp"),
            P("mp", None),
            P(None, "dp", None, "mp"),
            P(),
            P("dp"),
            P("dp"),
        ),
        out_specs=(P(None, "dp", "mp"), P("dp", None)),
        check_vma=False,
    )
```

profile of v0, /device:TPU:2, one launch (start us, length us, event | category | flops | bytes accessed | tf_op | source)
XLA Modules:
  0.0 589.8 jit_solution(4555764252407409945)
XLA Ops:
  11.2 24.7 %all-gather = bf16[512,1,128]{2,0,1:T(8,128)(2,1)S(1)} all-gather(bf16[16,1,128]{2,0,1:T(8,128)(2,1)S(1)} %copy.113), channel_id=2, replica_groups=mesh['dp'=32,'mp'=8] {'dp'}, dimensions={0}, use_global_device_ids=true | all-gather | bytes 135168 | tf_op jit(solution)/shard_map/all_gather | solution.py:64
  36.7 190.9 %while.35 = (s32[]{:T(128)}, f32[512,2]{0,1:T(2,128)S(1)}, f32[512,2]{0,1:T(2,128)S(1)}, f32[512,2,64]{0,2,1:T(8,128)S(1)}, s32[128]{0:T(128)S(1)}, /*index=5*/s...) while((s32[]{:T(128)}, f32[512,2]{0,1:T(2,128)S(1)}, ...), condition=%wide.region_6.7_spmd.clone.clone, body=%wide.region_2.6_spmd.clone.clone.sunk | while | flops 7361630 | bytes 5361311 | solution.py:127
  41.5 4.0 gather_fusion.2
  53.5 4.0 gather_fusion.2
  65.4 4.0 gather_fusion.2
  77.3 4.0 gather_fusion.2
  89.3 4.0 gather_fusion.2
  101.2 4.0 gather_fusion.2
  113.1 4.0 gather_fusion.2
  125.1 4.0 gather_fusion.2
  137.0 4.0 gather_fusion.2
  148.9 4.0 gather_fusion.2
  160.9 4.0 gather_fusion.2
  172.8 4.0 gather_fusion.2
  184.7 4.0 gather_fusion.2
  196.7 4.0 gather_fusion.2
  208.6 4.0 gather_fusion.2
  220.5 4.0 gather_fusion.2
  228.4 22.8 %all-gather.1 = f32[16384,2]{0,1:T(2,128)S(1)} all-gather(f32[512,2]{0,1:T(2,128)S(1)} %get-tuple-element.259), channel_id=3, replica_groups=mesh['dp'=32,'mp'=8] {'dp'}, dimensions={0}, use_global_device_ids=true | all-gather | bytes 135168 | tf_op jit(solution)/shard_map/all_gather | solution.py:13
  251.2 24.6 %all-gather.2 = f32[16384,2]{0,1:T(2,128)S(1)} all-gather(f32[512,2]{0,1:T(2,128)S(1)} %get-tuple-element.260), channel_id=4, replica_groups=mesh['dp'=32,'mp'=8] {'dp'}, dimensions={0}, use_global_device_ids=true | all-gather | bytes 135168 | tf_op jit(solution)/shard_map/all_gather | solution.py:13
  275.8 12.0 %all-gather.6.cloned.1.call-done = f32[16384,2,64]{0,2,1:T(8,128)} async-done(((f32[512,2,64]{0,2,1:T(8,128)}), f32[16384,2,64]{0,2,1:T(8,128)}) %all-gather.6.cloned.1.call-update) | async-done | bytes 8388624 | tf_op jit(solution)/shard_map/all_gather | solution.py:13
  289.0 7.1 %slice.95 = f32[15872,2,64]{0,2,1:T(8,128)} slice(f32[16384,2,64]{0,2,1:T(8,128)} %all-gather.6.cloned.1.call-done), slice={[512:16384], [0:2], [0:64]} | slice | bytes 16252928 | tf_op jit(solution)/shard_map/slice | solution.py:15
  296.1 19.6 %copy.125 = f32[15872,2,64]{2,1,0:T(2,128)} copy(f32[15872,2,64]{0,2,1:T(8,128)} %slice.95) | data formatting | bytes 16252928 | tf_op jit(solution)/shard_map/while | solution.py:16
  315.7 119.1 %while.34 = (s32[]{:T(128)}, f32[512,2]{0,1:T(2,128)S(1)}, f32[512,2]{0,1:T(2,128)S(1)}, f32[512,2,64]{2,1,0:T(2,128)S(1)}, f32[31,512,2]{1,2,0:T(2,128)S(1)}, /...) while((s32[]{:T(128)}, f32[512,2]{0,1:T(2,128)S(1)}, f32[512,2]{0,1:T(2,128)S(1)}, ...), condition=%wide.region_8.9_spmd, body=%wide.region_7.8_spmd.sunk | while | flops 202754 | bytes 843877 | solution.py:16
  316.0 3.5 fusion.67
  319.8 3.5 fusion.67
  323.7 3.5 fusion.67
  327.5 3.5 fusion.67
  331.4 3.5 fusion.67
  436.0 3.5 copy.128
  442.4 65.8 %all-reduce.3.cloned.1.call-done = f32[16,1024]{1,0:T(8,128)} async-done(((f32[16,1024]{1,0:T(8,128)}), f32[16,1024]{1,0:T(8,128)}) %all-reduce.3.cloned.1.call-update) | async-done | bytes 65552 | tf_op jit(solution)/shard_map/psum | solution.py:136
  511.4 70.4 %all-reduce.5.cloned.1.call-done = f32[16,1024]{1,0:T(8,128)} async-done(((f32[16,1024]{1,0:T(8,128)}), f32[16,1024]{1,0:T(8,128)}) %all-reduce.5.cloned.1.call-update) | async-done | bytes 65552 | tf_op jit(solution)/shard_map/psum | solution.py:148
  (672 shorter events, 240.6 us)
Async XLA Ops:
  7.2 502.7 %copy-start = (bf16[512,1024]{1,0:T(8,128)(2,1)S(1)}, bf16[512,1024]{1,0:T(8,128)(2,1)}, u32[]{:S(2)}) copy-start(bf16[512,1024]{1,0:T(8,128)(2,1)} %param.21) | copy-start | bytes 3145732
  7.2 280.6 %all-gather.6.cloned.1.call-start = ((), (), s32[]{:S(2)}) async-start(), calls=%async_computation.2 | async-start | bytes 8650752 | tf_op jit(solution)/shard_map/all_gather | solution.py:13
  227.6 0.7 copy-start.1
  228.3 279.9 %all-reduce.3.cloned.1.call-start = ((), (), s32[]{:S(2)}) async-start(), calls=%async_computation | async-start | bytes 131072 | tf_op jit(solution)/shard_map/psum | solution.py:136
  315.6 119.5 %copy-start.3 = (bf16[128,1024]{1,0:T(8,128)(2,1)S(1)}, bf16[128,1024]{1,0:T(8,128)(2,1)}, u32[]{:S(2)}) copy-start(bf16[128,1024]{1,0:T(8,128)(2,1)} %param.18) | copy-start | bytes 786436
  315.7 192.6 %copy-start.2 = (bf16[16,1024]{1,0:T(8,128)(2,1)S(1)}, bf16[16,1024]{1,0:T(8,128)(2,1)}, u32[]{:S(2)}) copy-start(bf16[16,1024]{1,0:T(8,128)(2,1)} %param.15) | copy-start | bytes 98308
  315.7 193.5 %copy-start.4 = (f32[1024]{0:T(1024)S(1)}, f32[1024]{0:T(1024)}, u32[]{:S(2)}) copy-start(f32[1024]{0:T(1024)} %param.19) | copy-start | bytes 12292
  436.0 145.8 %all-reduce.5.cloned.1.call-start = ((), (), s32[]{:S(2)}) async-start(), calls=%async_computation.1 | async-start | bytes 131072 | tf_op jit(solution)/shard_map/psum | solution.py:148
Sparse Core Ops, SparseCore 0:
  228.4 59.3 all-gather.5
  436.1 72.0 all-reduce.2
  510.9 70.8 all-reduce.4
where the time goes:
time: 593 us; the launch traced here: 590 us
  local copies, waits for them, and re-layouts  206 us (35%)
  waiting for transfers between devices  148 us (25%)
  other arithmetic  126 us (21%)
  blocking collectives  72.1 us (12%)
  matrix products  20.3 us (3%)
  between operations  13.9 us (2%)
    add x31, other arithmetic, combine(): first[2] * shrink_first[:, :, None] + second[2] * shrink_second[:, :, None]  108 us
    psum x1, waiting for transfers between devices, body(): lax.psum(jnp.dot(activated, w_down, preferred_element_type=jnp.float32),...  70.4 us
    psum x1, waiting for transfers between devices, body(): lax.psum(jnp.dot(context, w_out, preferred_element_type=jnp.float32), 'mp')  65.8 us
    gather x16, local copies, waits for them, and re-layouts, visit(): fetched = jnp.take(kv_cache, picked, axis=1)  64.4 us
    all_gather x2, blocking collectives, merged_2(): pieces = jax.tree.map(lambda part: lax.all_gather(part, axis), value)  47.4 us
    all_gather x1, blocking collectives, body(): every_query = lax.all_gather(projected[:, 0], 'dp', axis=0, tiled=True)  24.7 us
    gather x16, local copies, waits for them, and re-layouts, visit(): usable = (owners[:, None] >= 0) & (position < lengths[clamped][:, None])  21.2 us
    gather x16, local copies, waits for them, and re-layouts, visit(): owners = page_request[picked]  20.8 us
  transfers between devices with their start and end apart: 3, of which 3 were waited for; matrix products, arithmetic and copies ran while one was open for 1% of the time, Pallas kernels for 0%

commit v1 on v0

--- a/solution.py
+++ b/solution.py
@@ -2,6 +2,7 @@
 import jax.numpy as jnp
 from jax import lax
 from jax.sharding import PartitionSpec as P
+from jax.lax import all_gather
 
 HEAD_DIM = 64
 PAGE_BLOCK = 8
@@ -145,7 +146,11 @@
         preferred_element_type=jnp.float32,
     ).reshape(local_rows, 2, hidden_cols)
     activated = (jax.nn.silu(gate_up[:, 0]) * gate_up[:, 1]).astype(jnp.bfloat16)
-    lowered = lax.psum(jnp.dot(activated, w_down, preferred_element_type=jnp.float32), "mp")
+
+    def _treat_wall(xx):
+        return jnp.sum(all_gather(xx, "mp"), axis=0)
+
+    lowered = _treat_wall(jnp.dot(activated, w_down, preferred_element_type=jnp.float32))
     hidden_out = (residual.astype(jnp.float32) + lowered).astype(jnp.bfloat16)
     return (appended, hidden_out)
 

time: 593 us -> 548 us (0.924)
  waiting for transfers between devices: 148 us -> 78.9 us
  blocking collectives: 72.1 us -> 97.4 us
    psum x1 -> x0, waiting for transfers between devices: 70.4 us -> none  [body(): lax.psum(jnp.dot(activated, w_down, preferred_element_type=jnp.float32),...]
    all_gather x0 -> x1, blocking collectives: none -> 25.3 us  [_treat_wall(): return jnp.sum(all_gather(xx, 'mp'), axis=0)]
  transfers between devices with their start and end apart: 3 -> 2, of which waited for: 3 -> 2; matrix products, arithmetic and copies ran while one was open for 1% -> 1% of each run, Pallas kernels for 0% -> 0%
where the time goes in v1:
time: 548 us; the launch traced here: 544 us
  local copies, waits for them, and re-layouts  205 us (37%)
  other arithmetic  125 us (23%)
  blocking collectives  97.4 us (18%)
  waiting for transfers between devices  78.9 us (14%)
  matrix products  21.3 us (4%)
  between operations  14.2 us (3%)
    add x31, other arithmetic, combine(): first[2] * shrink_first[:, :, None] + second[2] * shrink_second[:, :, None]  108 us
    psum x1, waiting for transfers between devices, body(): lax.psum(jnp.dot(context, w_out, preferred_element_type=jnp.float32), 'mp')  71.6 us
    gather x16, local copies, waits for them, and re-layouts, visit(): fetched = jnp.take(kv_cache, picked, axis=1)  64.4 us
    all_gather x2, blocking collectives, merged_2(): pieces = jax.tree.map(lambda part: lax.all_gather(part, axis), value)  47.4 us
    all_gather x1, blocking collectives, _treat_wall(): return jnp.sum(all_gather(xx, 'mp'), axis=0)  25.3 us
    all_gather x1, blocking collectives, body(): every_query = lax.all_gather(projected[:, 0], 'dp', axis=0, tiled=True)  24.7 us
    gather x16, local copies, waits for them, and re-layouts, visit(): usable = (owners[:, None] >= 0) & (position < lengths[clamped][:, None])  21.2 us
    gather x16, local copies, waits for them, and re-layouts, visit(): owners = page_request[picked]  20.8 us
  transfers between devices with their start and end apart: 2, of which 2 were waited for; matrix products, arithmetic and copies ran while one was open for 1% of the time, Pallas kernels for 0%

profile of v1, /device:TPU:2, one launch (start us, length us, event | category | flops | bytes accessed | tf_op | source)
XLA Modules:
  0.0 544.5 jit_solution(3065400921297633124)
XLA Ops:
  11.2 24.7 %all-gather = bf16[512,1,128]{2,0,1:T(8,128)(2,1)S(1)} all-gather(bf16[16,1,128]{2,0,1:T(8,128)(2,1)S(1)} %copy.113), channel_id=2, replica_groups=mesh['dp'=32,'mp'=8] {'dp'}, dimensions={0}, use_global_device_ids=true | all-gather | bytes 135168 | tf_op jit(solution)/shard_map/all_gather | solution.py:65
  36.7 190.9 %while.35 = (s32[]{:T(128)}, f32[512,2]{0,1:T(2,128)S(1)}, f32[512,2]{0,1:T(2,128)S(1)}, f32[512,2,64]{0,2,1:T(8,128)S(1)}, s32[128]{0:T(128)S(1)}, /*index=5*/s...) while((s32[]{:T(128)}, f32[512,2]{0,1:T(2,128)S(1)}, ...), condition=%wide.region_6.7_spmd.clone.clone, body=%wide.region_2.6_spmd.clone.clone.sunk | while | flops 7361630 | bytes 5361311 | solution.py:128
  41.5 4.0 gather_fusion.2
  53.5 4.0 gather_fusion.2
  65.4 4.0 gather_fusion.2
  77.3 4.0 gather_fusion.2
  89.3 4.0 gather_fusion.2
  101.2 4.0 gather_fusion.2
  113.1 4.0 gather_fusion.2
  125.1 4.0 gather_fusion.2
  137.0 4.0 gather_fusion.2
  148.9 4.0 gather_fusion.2
  160.9 4.0 gather_fusion.2
  172.8 4.0 gather_fusion.2
  184.7 4.0 gather_fusion.2
  196.7 4.0 gather_fusion.2
  208.6 4.0 gather_fusion.2
  220.5 4.0 gather_fusion.2
  228.4 22.8 %all-gather.1 = f32[16384,2]{0,1:T(2,128)S(1)} all-gather(f32[512,2]{0,1:T(2,128)S(1)} %get-tuple-element.259), channel_id=3, replica_groups=mesh['dp'=32,'mp'=8] {'dp'}, dimensions={0}, use_global_device_ids=true | all-gather | bytes 135168 | tf_op jit(solution)/shard_map/all_gather | solution.py:14
  251.2 24.6 %all-gather.2 = f32[16384,2]{0,1:T(2,128)S(1)} all-gather(f32[512,2]{0,1:T(2,128)S(1)} %get-tuple-element.260), channel_id=4, replica_groups=mesh['dp'=32,'mp'=8] {'dp'}, dimensions={0}, use_global_device_ids=true | all-gather | bytes 135168 | tf_op jit(solution)/shard_map/all_gather | solution.py:14
  280.6 7.2 %all-gather.7.cloned.1.call-done = f32[16384,2,64]{0,2,1:T(8,128)} async-done(((f32[512,2,64]{0,2,1:T(8,128)}), f32[16384,2,64]{0,2,1:T(8,128)}) %all-gather.7.cloned.1.call-update) | async-done | bytes 8388624 | tf_op jit(solution)/shard_map/all_gather | solution.py:14
  289.0 7.1 %slice.95 = f32[15872,2,64]{0,2,1:T(8,128)} slice(f32[16384,2,64]{0,2,1:T(8,128)} %all-gather.7.cloned.1.call-done), slice={[512:16384], [0:2], [0:64]} | slice | bytes 16252928 | tf_op jit(solution)/shard_map/slice | solution.py:16
  296.1 19.6 %copy.125 = f32[15872,2,64]{2,1,0:T(2,128)} copy(f32[15872,2,64]{0,2,1:T(8,128)} %slice.95) | data formatting | bytes 16252928 | tf_op jit(solution)/shard_map/while | solution.py:17
  315.7 119.1 %while.34 = (s32[]{:T(128)}, f32[512,2]{0,1:T(2,128)S(1)}, f32[512,2]{0,1:T(2,128)S(1)}, f32[512,2,64]{2,1,0:T(2,128)S(1)}, f32[31,512,2]{1,2,0:T(2,128)S(1)}, /...) while((s32[]{:T(128)}, f32[512,2]{0,1:T(2,128)S(1)}, f32[512,2]{0,1:T(2,128)S(1)}, ...), condition=%wide.region_8.9_spmd, body=%wide.region_7.8_spmd.sunk | while | flops 202754 | bytes 843877 | solution.py:17
  316.0 3.5 fusion.67
  319.8 3.5 fusion.67
  323.7 3.5 fusion.67
  327.5 3.5 fusion.67
  331.4 3.5 fusion.67
  335.2 3.5 fusion.67
  436.6 71.6 %all-reduce.2.cloned.1.call-done = f32[16,1024]{1,0:T(8,128)} async-done(((f32[16,1024]{1,0:T(8,128)}), f32[16,1024]{1,0:T(8,128)}) %all-reduce.2.cloned.1.call-update) | async-done | bytes 65552 | tf_op jit(solution)/shard_map/psum | solution.py:137
  511.7 25.3 %all-gather.4 = f32[128,1024]{1,0:T(8,128)S(1)} all-gather(f32[16,1024]{1,0:T(8,128)S(1)} %fusion.35), channel_id=6, replica_groups=mesh['dp'=32,'mp'=8] {'mp'}, dimensions={0}, use_global_device_ids=true | all-gather | bytes 589824 | tf_op jit(solution)/shard_map/all_gather | solution.py:151
  (671 shorter events, 239.2 us)
Async XLA Ops:
  7.2 504.3 %copy-start = (bf16[512,1024]{1,0:T(8,128)(2,1)S(1)}, bf16[512,1024]{1,0:T(8,128)(2,1)}, u32[]{:S(2)}) copy-start(bf16[512,1024]{1,0:T(8,128)(2,1)} %param.21) | copy-start | bytes 3145732
  7.2 280.6 %all-gather.7.cloned.1.call-start = ((), (), s32[]{:S(2)}) async-start(), calls=%async_computation.1 | async-start | bytes 8650752 | tf_op jit(solution)/shard_map/all_gather | solution.py:14
  227.6 0.7 copy-start.1
  228.3 279.9 %all-reduce.2.cloned.1.call-start = ((), (), s32[]{:S(2)}) async-start(), calls=%async_computation | async-start | bytes 131072 | tf_op jit(solution)/shard_map/psum | solution.py:137
  315.6 119.5 %copy-start.3 = (bf16[128,1024]{1,0:T(8,128)(2,1)S(1)}, bf16[128,1024]{1,0:T(8,128)(2,1)}, u32[]{:S(2)}) copy-start(bf16[128,1024]{1,0:T(8,128)(2,1)} %param.18) | copy-start | bytes 786436
  315.7 192.6 %copy-start.2 = (bf16[16,1024]{1,0:T(8,128)(2,1)S(1)}, bf16[16,1024]{1,0:T(8,128)(2,1)}, u32[]{:S(2)}) copy-start(bf16[16,1024]{1,0:T(8,128)(2,1)} %param.15) | copy-start | bytes 98308
  315.7 193.5 %copy-start.4 = (f32[1024]{0:T(1024)S(1)}, f32[1024]{0:T(1024)}, u32[]{:S(2)}) copy-start(f32[1024]{0:T(1024)} %param.19) | copy-start | bytes 12292
Sparse Core Ops, SparseCore 0:
  228.4 59.3 all-gather.6
  436.1 72.0 all-reduce.1
